TPU v7x, 32 devices: a whole 2x2x4 slice. The times are simulated.
32 devices in a mesh: dp: 2 (over y), expert: 16 (over z, x, core).
Axes of the slice: x: 2, y: 2, z: 4, core: 2. Of those that a mesh axis runs over, the one named last changes fastest.
Arguments:
- tokens: bfloat16 [2048, 1024], P(('dp', 'expert')), may hold values from -6 to 6
- cotangent: bfloat16 [2048, 1024], P(('dp', 'expert')), may hold values from -6 to 6
- expert_ids: int32 [2048, 6], P(('dp', 'expert')), may hold values from 0 to 15, all different within a row; in each aligned block of 64 rows (0 to 63, 64 to 127, ...) at most 32 rows name the same one
- gate_probs: float32 [2048, 6], P(('dp', 'expert')), may hold values from 0.1 to 1
- w_gate_up: bfloat16 [16, 1024, 1408], P('expert', 'dp'), may hold values from -0.1875 to 0.1875
- w_down: bfloat16 [16, 704, 1024], P('expert'), may hold values from -0.21875 to 0.21875
Outputs:
- layer_out: bfloat16 [2048, 1024], P(('dp', 'expert'))
- input_grad: bfloat16 [2048, 1024], P(('dp', 'expert'))
- prob_grad: float32 [2048, 6], P(('dp', 'expert'))
- gate_up_grad: bfloat16 [16, 1024, 1408], P('expert', 'dp')
Inputs may be any that keep to these rules, and one draw needn't show every extreme that they name: `expert_ids`: each row names 6 different experts. Within each aligned block of 64 rows no expert is named by more than 32 rows, and in some block an expert is named by exactly 32 rows.
All inputs are finite; a program needn't handle non-finite values.
Results may differ from a plain program's by a relative error of at most 0.013.
Values may be sent and summed in bfloat16 or wider, within the bound.
No kernel may reach another device: no remote copies, remote signals or barrier semaphores. Data moves between devices by JAX's collectives and lax.ppermute only.
A program may use at most 64 MiB of HBM per device.

v0:
```python
import jax
import jax.numpy as jnp
from jax import lax
from jax.sharding import PartitionSpec as P


def local(tokens, cotangent, expert_ids, gate_probs, w_gate_up, w_down):
    experts = lax.axis_size("expert")
    token_count = tokens.shape[0]
    model_width = tokens.shape[1]
    top_count = expert_ids.shape[1]
    hidden_units = w_down.shape[1]
    capacity = 4 * token_count * top_count // (3 * experts)
    flat_routes = expert_ids.reshape(token_count * top_count)
    onehot = (flat_routes[:, None] == jnp.arange(experts, dtype=jnp.int32)[None, :]).astype(
        jnp.int32
    )
    before = jnp.cumsum(onehot, axis=0) - onehot
    slot_rank = jnp.sum(before * onehot, axis=1)
    target_rows = flat_routes * capacity + slot_rank
    token_copies = jnp.broadcast_to(tokens[:, None, :], (token_count, top_count, model_width))
    token_copies = token_copies.reshape(token_count * top_count, model_width)
    cot_copies = (gate_probs[:, :, None] * cotangent[:, None, :].astype(jnp.float32)).astype(
        jnp.bfloat16
    )
    cot_copies = cot_copies.reshape(token_count * top_count, model_width)
    token_send = (
        jnp.zeros((experts * capacity, model_width), jnp.bfloat16).at[target_rows].set(token_copies)
    )
    cot_send = (
        jnp.zeros((experts * capacity, model_width), jnp.bfloat16).at[target_rows].set(cot_copies)
    )
    token_send = token_send.reshape(experts, capacity, model_width)
    cot_send = cot_send.reshape(experts, capacity, model_width)
    token_recv, cot_early = (
        lax.all_to_all(token_send, "expert", split_axis=0, concat_axis=0, tiled=True),
        lax.all_to_all(cot_send, "expert", split_axis=0, concat_axis=0, tiled=True),
    )
    input_rows = token_recv.reshape(experts * capacity, model_width)
    weight_down = w_down[0]
    weight_fwd = lax.all_gather(w_gate_up, "dp", axis=1, tiled=True)[0]
    gate_up = jnp.dot(input_rows, weight_fwd, preferred_element_type=jnp.float32)
    gate = gate_up[:, :hidden_units]
    upper = gate_up[:, hidden_units:]
    sigma = jax.nn.sigmoid(gate)
    active = gate * sigma
    hidden = (active * upper).astype(jnp.bfloat16)
    output_rows = jnp.dot(hidden, weight_down, preferred_element_type=jnp.float32).astype(
        jnp.bfloat16
    )
    cot_rows = cot_early.reshape(experts * capacity, model_width)
    hidden_grad = lax.dot_general(
        cot_rows, weight_down, (((1,), (1,)), ((), ())), preferred_element_type=jnp.float32
    )
    gate_cot = hidden_grad * upper * sigma * (1.0 + gate * (1.0 - sigma))
    upper_cot = hidden_grad * active
    pair_cot = jnp.concatenate([gate_cot, upper_cot], axis=1).astype(jnp.bfloat16)
    input_cot = lax.dot_general(
        pair_cot, weight_fwd, (((1,), (1,)), ((), ())), preferred_element_type=jnp.float32
    ).astype(jnp.bfloat16)
    weight_cot = lax.dot_general(
        input_rows, pair_cot, (((0,), (0,)), ((), ())), preferred_element_type=jnp.float32
    )
    output_back, input_back = (
        lax.all_to_all(
            output_rows.reshape(experts, capacity, model_width),
            "expert",
            split_axis=0,
            concat_axis=0,
            tiled=True,
        ),
        lax.all_to_all(
            input_cot.reshape(experts, capacity, model_width),
            "expert",
            split_axis=0,
            concat_axis=0,
            tiled=True,
        ),
    )
    slot_out = output_back.reshape(experts * capacity, model_width)[target_rows].reshape(
        token_count, top_count, model_width
    )
    slot_in = input_back.reshape(experts * capacity, model_width)[target_rows].reshape(
        token_count, top_count, model_width
    )
    layer_out = jnp.sum(gate_probs[:, :, None] * slot_out.astype(jnp.float32), axis=1).astype(
        jnp.bfloat16
    )
    input_grad = jnp.sum(slot_in.astype(jnp.float32), axis=1).astype(jnp.bfloat16)
    prob_grad = jnp.einsum("td,tkd->tk", cotangent, slot_out, preferred_element_type=jnp.float32)
    grad_rows = lax.psum_scatter(
        weight_cot.astype(jnp.bfloat16), "dp", scatter_dimension=0, tiled=True
    )
    return (layer_out, input_grad, prob_grad, grad_rows[None])


def solution(mesh):
    placed = (
        P(("dp", "expert"), None),
        P(("dp", "expert"), None),
        P(("dp", "expert"), None),
        P(("dp", "expert"), None),
        P("expert", "dp", None),
        P("expert", None, None),
    )
    return jax.shard_map(
        local,
        mesh=mesh,
        in_specs=placed,
        out_specs=(
            P(("dp", "expert"), None),
            P(("dp", "expert"), None),
            P(("dp", "expert"), None),
            P("expert", "dp", None),
        ),
        check_vma=False,
    )
```

profile of v0, /device:TPU:15, one launch (start us, length us, event | category | flops | bytes accessed | tf_op | source)
XLA Modules:
  0.0 166.2 jit_solution(6136234102006525579)
XLA Ops:
  7.2 0.0 copy-start
  7.2 0.8 broadcast_multiply_fusion
  8.0 0.8 copy.15
  8.8 0.1 eq.29
  8.9 0.1 eq.25
  9.0 0.1 copy.14
  9.1 0.1 mul.69
  9.3 0.9 reduce-window.6
  10.2 0.2 slice_reduce_fusion
  10.4 1.1 broadcast_in_dim.4
  11.5 0.3 reshape.126
  11.8 0.1 fusion.21
  11.9 3.1 %scatter_custom_fusion = bf16[512,1024]{1,0:T(8,128)(2,1)} fusion(s32[384]{0:T(512)S(1)} %fusion.23, bf16[384,1024]{1,0:T(8,128)(2,1)S(1)} %reshape.126, bf16[]{:T(256)} %constant.6.clone.1), kind=kCustom, calls=%fused_computation.25 | custom fusion | bytes 1048578 | tf_op jit(solution)/shard_map/scatter | solution.py:28
  15.0 0.0 copy-start.3
  15.0 6.7 %all-to-all-start = ((bf16[16,32,1024]{2,1,0:T(8,128)(2,1)}), bf16[16,32,1024]{2,1,0:T(8,128)(2,1)}, u32[]{:S(2)}, u32[]{:S(2)}) async-start(bf16[16,32,1024]{2,1,0:T(8,128)(2,1)} %bitcast.1), calls=%async_computation | async-start | bytes 2097152 | tf_op jit(solution)/shard_map/all_to_all | solution.py:36
  21.7 0.0 all-gather.2.cloned.1.call-start
  21.7 0.7 all-gather.2.cloned.1.call-update
  22.4 0.0 copy-done.3
  22.4 0.1 copy.13
  22.5 0.0 copy-start.1
  22.5 0.6 copy-done.1
  23.1 0.1 mul.74
  23.2 1.2 mul.76
  24.4 1.4 mul.77
  25.8 4.0 %scatter_custom_fusion.1 = bf16[512,1024]{1,0:T(8,128)(2,1)} fusion(s32[384]{0:T(512)S(1)} %fusion.23, f32[384,1024]{1,0:T(8,128)} %mul.77, f32[384]{0:T(512)S(1)} %mul.74, bf16[]{:T(256)} %constant.6.clone.1), kind=kCustom, calls=%fused_computation.22 | custom fusion | flops 786432 | bytes 2623490 | tf_op jit(solution)/shard_map/scatter | solution.py:31
  29.8 17.2 %all-to-all-done = bf16[16,32,1024]{2,1,0:T(8,128)(2,1)} async-done(((bf16[16,32,1024]{2,1,0:T(8,128)(2,1)}), bf16[16,32,1024]{2,1,0:T(8,128)(2,1)}, u32[]{:S(2)}, u32[]{:S(2)}) %all-to-all-start) | async-done | bytes 1048608 | tf_op jit(solution)/shard_map/all_to_all | solution.py:36
  46.9 4.6 %all-to-all-start.2 = ((bf16[16,32,1024]{2,1,0:T(8,128)(2,1)}), bf16[16,32,1024]{2,1,0:T(8,128)(2,1)S(1)}, u32[]{:S(2)}, u32[]{:S(2)}) async-start(bf16[16,32,1024]{2,1,0:T(8,128)(2,1)} %bitcast.7), calls=%async_computation.2 | async-start | bytes 2097152 | tf_op jit(solution)/shard_map/all_to_all | solution.py:37
  51.6 0.0 reduce-scatter.2.cloned.1.call-start
  51.6 14.1 %all-gather.2.cloned.1.call-done = bf16[1,1024,1408]{2,1,0:T(8,128)(2,1)} async-done(((bf16[1,512,1408]{2,1,0:T(8,128)(2,1)}), bf16[1,1024,1408]{2,1,0:T(8,128)(2,1)}) %all-gather.2.cloned.1.call-update) | async-done | bytes 2883600 | tf_op jit(solution)/shard_map/all_gather | solution.py:41
  65.7 5.5 %fusion.2 = f32[512,1408]{1,0:T(8,128)} fusion(bf16[512,1024]{1,0:T(8,128)(2,1)} %bitcast.2, bf16[1,1024,1408]{2,1,0:T(8,128)(2,1)} %all-gather.2.cloned.1.call-done), kind=kOutput, calls=%fused_computation.7 | convolution fusion | flops 1476395008 | bytes 6815744 | tf_op jit(solution)/shard_map/dot_general | solution.py:42
  71.2 5.3 %all-to-all-done.2 = bf16[16,32,1024]{2,1,0:T(8,128)(2,1)S(1)} async-done(((bf16[16,32,1024]{2,1,0:T(8,128)(2,1)}), bf16[16,32,1024]{2,1,0:T(8,128)(2,1)S(1)}, u32[]{:S(2)}, u32[]{:S(2)}) %all-to-all-start.2) | async-done | bytes 1048608 | tf_op jit(solution)/shard_map/all_to_all | solution.py:37
  76.5 0.0 copy-done
  76.5 3.3 %multiply_convert_fusion.1 = (bf16[512,704]{1,0:T(8,128)(2,1)S(1)}, bf16[512,704]{1,0:T(8,128)(2,1)S(1)}) fusion(f32[512,1408]{1,0:T(8,128)} %fusion.2, bf16[512,1024]{1,0:T(8,128)(2,1)S(1)} %bitcast.53, bf16[1,704,1024]{2,1,0:T(8,128)(2,1)S(1)} %copy-done), kind=kOutput, calls=%fused_computation.11 | convolution fusion | flops 742883328 | bytes 6815744 | tf_op jit(solution)/shard_map/dot_general | solution.py:52
  79.8 0.0 copy-start.4
  79.8 0.9 copy-done.4
  80.7 4.7 %convolution_convert_fusion = bf16[1024,1408]{1,0:T(8,128)(2,1)} fusion(bf16[512,1024]{1,0:T(8,128)(2,1)} %bitcast.2, bf16[512,704]{1,0:T(8,128)(2,1)S(1)} %get-tuple-element.5, bf16[512,704]{1,0:T(8,128)(2,1)S(1)} %get-tuple-element.4), kind=kOutput, calls=%fused_computation.4 | convolution fusion | flops 1480720384 | bytes 5373952 | tf_op jit(solution)/shard_map/dot_general | solution.py:61
  85.3 0.0 reduce-scatter.2.cloned.1.call-update
  85.4 4.0 %convolution_convert_fusion.1 = bf16[512,1024]{1,0:T(8,128)(2,1)} fusion(bf16[1,704,1024]{2,1,0:T(8,128)(2,1)S(1)} %copy-done, f32[512,1408]{1,0:T(8,128)} %fusion.2), kind=kOutput, calls=%fused_computation.17 | convolution fusion | flops 740884480 | bytes 5636096 | tf_op jit(solution)/shard_map/dot_general | solution.py:48
  89.3 4.9 %all-to-all-start.1 = ((bf16[16,32,1024]{2,1,0:T(8,128)(2,1)}), bf16[16,32,1024]{2,1,0:T(8,128)(2,1)S(1)}, u32[]{:S(2)}, u32[]{:S(2)}) async-start(bf16[16,32,1024]{2,1,0:T(8,128)(2,1)} %bitcast.5), calls=%async_computation.1 | async-start | bytes 2097152 | tf_op jit(solution)/shard_map/all_to_all | solution.py:65
  94.3 4.9 %fusion.5 = bf16[512,1024]{1,0:T(8,128)(2,1)} fusion(bf16[1,1024,1408]{2,1,0:T(8,128)(2,1)} %all-gather.2.cloned.1.call-done, bf16[512,704]{1,0:T(8,128)(2,1)} %copy-done.4, bf16[512,704]{1,0:T(8,128)(2,1)S(1)} %get-tuple-element.4), kind=kOutput, calls=%fused_computation.16 | convolution fusion | flops 1479802880 | bytes 5373952 | tf_op jit(solution)/shard_map/dot_general | solution.py:58
  99.2 20.4 %all-to-all-done.1 = bf16[16,32,1024]{2,1,0:T(8,128)(2,1)S(1)} async-done(((bf16[16,32,1024]{2,1,0:T(8,128)(2,1)}), bf16[16,32,1024]{2,1,0:T(8,128)(2,1)S(1)}, u32[]{:S(2)}, u32[]{:S(2)}) %all-to-all-start.1) | async-done | bytes 1048608 | tf_op jit(solution)/shard_map/all_to_all | solution.py:65
  119.6 4.5 %all-to-all-start.3 = ((bf16[16,32,1024]{2,1,0:T(8,128)(2,1)}), bf16[16,32,1024]{2,1,0:T(8,128)(2,1)S(1)}, u32[]{:S(2)}, u32[]{:S(2)}) async-start(bf16[16,32,1024]{2,1,0:T(8,128)(2,1)} %bitcast.54), calls=%async_computation.3 | async-start | bytes 2097152 | tf_op jit(solution)/shard_map/all_to_all | solution.py:72
  124.1 2.7 %gather_fusion = bf16[384,1024]{1,0:T(8,128)(2,1)} fusion(bf16[512,1024]{1,0:T(8,128)(2,1)S(1)} %bitcast.51, s32[1024]{0:T(1024)S(1)} %pad_clamp_fusion), kind=kCustom, calls=%fused_computation | custom fusion | bytes 1574400 | tf_op jit(solution)/shard_map/gather | solution.py:80
  126.8 22.2 %all-to-all-done.3 = bf16[16,32,1024]{2,1,0:T(8,128)(2,1)S(1)} async-done(((bf16[16,32,1024]{2,1,0:T(8,128)(2,1)}), bf16[16,32,1024]{2,1,0:T(8,128)(2,1)S(1)}, u32[]{:S(2)}, u32[]{:S(2)}) %all-to-all-start.3) | async-done | bytes 1048608 | tf_op jit(solution)/shard_map/all_to_all | solution.py:72
  149.0 2.7 %gather_fusion.1 = bf16[384,1024]{1,0:T(8,128)(2,1)} fusion(bf16[512,1024]{1,0:T(8,128)(2,1)S(1)} %bitcast.52, s32[1024]{0:T(1024)S(1)} %pad_clamp_fusion), kind=kCustom, calls=%fused_computation.1 | custom fusion | bytes 1574400 | tf_op jit(solution)/shard_map/gather | solution.py:83
  151.6 0.0 copy-start.2
  151.6 1.4 reshape.100
  153.0 0.0 copy-done.2
  153.0 0.7 fusion.16
  153.8 0.7 copy.23
  154.4 1.3 reshape.105
  155.8 1.4 reduce_sum.35
  157.1 2.2 %multiply_reduce_fusion = bf16[64,1024]{1,0:T(8,128)(2,1)} fusion(bf16[64,6,1024]{2,1,0:T(8,128)(2,1)S(1)} %reshape.100, f32[64,6]{1,0:T(8,128)} %copy-done.1), kind=kLoop, calls=%fused_computation.9 | loop fusion | flops 1114112 | bytes 919040 | tf_op jit(solution)/shard_map/reduce_sum | solution.py:86
  159.3 0.0 reduce-scatter.2.cloned.1.call-done
  (4 shorter events, 0.1 us)
Async XLA Ops:
  7.2 69.3 %copy-start = (bf16[1,704,1024]{2,1,0:T(8,128)(2,1)S(1)}, bf16[1,704,1024]{2,1,0:T(8,128)(2,1)}, u32[]{:S(2)}) copy-start(bf16[1,704,1024]{2,1,0:T(8,128)(2,1)} %param.11) | copy-start | bytes 4325380
  15.0 7.4 %copy-start.3 = (f32[64,6]{0,1:T(8,128)S(1)}, f32[64,6]{0,1:T(8,128)}, u32[]{:S(2)}) copy-start(f32[64,6]{0,1:T(8,128)} %param.9) | copy-start | bytes 4612
  15.0 32.0 %all-to-all-start = ((bf16[16,32,1024]{2,1,0:T(8,128)(2,1)}), bf16[16,32,1024]{2,1,0:T(8,128)(2,1)}, u32[]{:S(2)}, u32[]{:S(2)}) async-start(bf16[16,32,1024]{2,1,0:T(8,128)(2,1)} %bitcast.1), calls=%async_computation | async-start | bytes 2097152 | tf_op jit(solution)/shard_map/all_to_all | solution.py:36
  21.7 44.0 %all-gather.2.cloned.1.call-start = ((), (), s32[]{:S(2)}) async-start(), calls=%async_computation.5 | async-start | bytes 4325376 | tf_op jit(solution)/shard_map/all_gather | solution.py:41
  22.5 0.6 copy-start.1
  46.9 29.5 %all-to-all-start.2 = ((bf16[16,32,1024]{2,1,0:T(8,128)(2,1)}), bf16[16,32,1024]{2,1,0:T(8,128)(2,1)S(1)}, u32[]{:S(2)}, u32[]{:S(2)}) async-start(bf16[16,32,1024]{2,1,0:T(8,128)(2,1)} %bitcast.7), calls=%async_computation.2 | async-start | bytes 2097152 | tf_op jit(solution)/shard_map/all_to_all | solution.py:37
  51.6 107.8 %reduce-scatter.2.cloned.1.call-start = ((), (), s32[]{:S(2)}) async-start(), calls=%async_computation.6 | async-start | bytes 4325376 | tf_op jit(solution)/shard_map/reduce_scatter | solution.py:91
  79.8 0.9 copy-start.4
  89.3 30.2 %all-to-all-start.1 = ((bf16[16,32,1024]{2,1,0:T(8,128)(2,1)}), bf16[16,32,1024]{2,1,0:T(8,128)(2,1)S(1)}, u32[]{:S(2)}, u32[]{:S(2)}) async-start(bf16[16,32,1024]{2,1,0:T(8,128)(2,1)} %bitcast.5), calls=%async_computation.1 | async-start | bytes 2097152 | tf_op jit(solution)/shard_map/all_to_all | solution.py:65
  119.6 29.4 %all-to-all-start.3 = ((bf16[16,32,1024]{2,1,0:T(8,128)(2,1)}), bf16[16,32,1024]{2,1,0:T(8,128)(2,1)S(1)}, u32[]{:S(2)}, u32[]{:S(2)}) async-start(bf16[16,32,1024]{2,1,0:T(8,128)(2,1)} %bitcast.54), calls=%async_computation.3 | async-start | bytes 2097152 | tf_op jit(solution)/shard_map/all_to_all | solution.py:72
  151.6 1.4 copy-start.2
Sparse Core Ops, SparseCore 0:
  24.0 41.6 all-gather.1
  85.5 39.0 reduce-scatter.1
where the time goes:
time: 167 us; the launch traced here: 166 us
  waiting for transfers between devices  79.7 us (48%)
  matrix products  23 us (14%)
  starting transfers between devices  20.9 us (13%)
  local copies, waits for them, and re-layouts  18.9 us (11%)
  between operations  14.2 us (9%)
  other arithmetic  9.39 us (6%)
    all_to_all x1, waiting for transfers between devices, local(): lax.all_to_all(input_cot.reshape(experts, capacity, model_width), 'expert...  22.2 us
    all_to_all x1, waiting for transfers between devices, local(): lax.all_to_all(output_rows.reshape(experts, capacity, model_width), 'expe...  20.4 us
    all_to_all x1, waiting for transfers between devices, local(): lax.all_to_all(token_send, 'expert', split_axis=0, concat_axis=0, tiled=T...  17.2 us
    all_gather x1, waiting for transfers between devices, local(): weight_fwd = lax.all_gather(w_gate_up, 'dp', axis=1, tiled=True)[0]  14.1 us
    all_to_all x1, starting transfers between devices, local(): lax.all_to_all(token_send, 'expert', split_axis=0, concat_axis=0, tiled=T...  6.69 us
    dot_general x1, matrix products, local(): jnp.dot(input_rows, weight_fwd, preferred_element_type=jnp.float32)  5.5 us
    all_to_all x1, waiting for transfers between devices, local(): lax.all_to_all(cot_send, 'expert', split_axis=0, concat_axis=0, tiled=True)  5.26 us
    all_to_all x1, starting transfers between devices, local(): lax.all_to_all(output_rows.reshape(experts, capacity, model_width), 'expe...  4.95 us
  transfers between devices with their start and end apart: 6, of which 5 were waited for; matrix products, arithmetic and copies ran while one was open for 21% of the time, Pallas kernels for 0%

commit v1 on v0

--- a/solution.py
+++ b/solution.py
@@ -2,6 +2,39 @@
 import jax.numpy as jnp
 from jax import lax
 from jax.sharding import PartitionSpec as P
+from jax.lax import axis_index, ppermute, psum
+
+
+def work_the_group(target, array_dim, values):
+    value_now = target.shape
+    moved = target.reshape(
+        *value_now[:array_dim], values, value_now[array_dim] // values, *value_now[array_dim + 1 :]
+    )
+    return jnp.moveaxis(moved, array_dim, 0)
+
+
+def work_page(mine_x, dim_at):
+    f_now = list(mine_x.shape[1:])
+    f_now[dim_at] *= mine_x.shape[0]
+    return jnp.moveaxis(mine_x, 0, dim_at).reshape(f_now)
+
+
+def set_the_copies(chunk, comm_axis, unit, arr):
+    tile_out = psum(1, axis_name=comm_axis)
+    arr_now, piece_now = (tile_out, axis_index(comm_axis))
+    seen_now = work_the_group(chunk, unit, arr_now)
+    entries = [seen_now[piece_now]]
+    for num in range(1, arr_now):
+        plain = seen_now[(piece_now + num) % arr_now]
+        entries.append(
+            ppermute(
+                plain,
+                axis_name=comm_axis,
+                perm=[(dev_i, (dev_i + num) % arr_now) for dev_i in range(arr_now)],
+            )
+        )
+    seen_now = jnp.stack(entries)[(piece_now - jnp.arange(arr_now)) % arr_now]
+    return work_page(seen_now, arr)
 
 
 def local(tokens, cotangent, expert_ids, gate_probs, w_gate_up, w_down):
@@ -33,7 +66,7 @@
     token_send = token_send.reshape(experts, capacity, model_width)
     cot_send = cot_send.reshape(experts, capacity, model_width)
     token_recv, cot_early = (
-        lax.all_to_all(token_send, "expert", split_axis=0, concat_axis=0, tiled=True),
+        set_the_copies(token_send, "expert", 0, 0),
         lax.all_to_all(cot_send, "expert", split_axis=0, concat_axis=0, tiled=True),
     )
     input_rows = token_recv.reshape(experts * capacity, model_width)

time: 167 us -> 208 us (1.25)
  starting transfers between devices: 20.9 us -> 48.4 us
  waiting for transfers between devices: 79.7 us -> 90.9 us
  local copies, waits for them, and re-layouts: 18.9 us -> 22.9 us
    ppermute x0 -> x15, waiting for transfers between devices: none -> 47.6 us  [set_the_copies(): ppermute(plain, axis_name=comm_axis, perm=[(dev_i, (dev_i + num) % arr_no...]
    ppermute x0 -> x15, starting transfers between devices: none -> 32.5 us  [set_the_copies(): ppermute(plain, axis_name=comm_axis, perm=[(dev_i, (dev_i + num) % arr_no...]
    all_to_all x1 -> x0, waiting for transfers between devices: 17.2 us -> none  [local(): lax.all_to_all(token_send, 'expert', split_axis=0, concat_axis=0, tiled=T...]
    all_gather x1, waiting for transfers between devices: 14.1 us -> 0.02 us  [local(): weight_fwd = lax.all_gather(w_gate_up, 'dp', axis=1, tiled=True)[0]]
    all_to_all x1 -> x0, starting transfers between devices: 6.69 us -> none  [local(): lax.all_to_all(token_send, 'expert', split_axis=0, concat_axis=0, tiled=T...]
    all_to_all x1, waiting for transfers between devices: 5.26 us -> 0.01 us  [local(): lax.all_to_all(cot_send, 'expert', split_axis=0, concat_axis=0, tiled=True)]
    unnamed x12 -> x56, local copies, waits for them, and re-layouts: 2.38 us -> 5.43 us
  transfers between devices with their start and end apart: 6 -> 20, of which waited for: 5 -> 12; matrix products, arithmetic and copies ran while one was open for 21% -> 21% of each run, Pallas kernels for 0% -> 0%
where the time goes in v1:
time: 208 us; the launch traced here: 207 us
  waiting for transfers between devices  90.9 us (44%)
  starting transfers between devices  48.4 us (23%)
  local copies, waits for them, and re-layouts  22.9 us (11%)
  matrix products  21.9 us (11%)
  between operations  14.6 us (7%)
  other arithmetic  8.67 us (4%)
    ppermute x15, waiting for transfers between devices, set_the_copies(): ppermute(plain, axis_name=comm_axis, perm=[(dev_i, (dev_i + num) % arr_no...  47.6 us
    ppermute x15, starting transfers between devices, set_the_copies(): ppermute(plain, axis_name=comm_axis, perm=[(dev_i, (dev_i + num) % arr_no...  32.5 us
    all_to_all x1, waiting for transfers between devices, local(): lax.all_to_all(input_cot.reshape(experts, capacity, model_width), 'expert...  22.2 us
    all_to_all x1, waiting for transfers between devices, local(): lax.all_to_all(output_rows.reshape(experts, capacity, model_width), 'expe...  20.4 us
    all_to_all x1, starting transfers between devices, local(): lax.all_to_all(output_rows.reshape(experts, capacity, model_width), 'expe...  6.47 us
    unnamed x56, local copies, waits for them, and re-layouts  5.43 us
    dot_general x1, matrix products, local(): jnp.dot(input_rows, weight_fwd, preferred_element_type=jnp.float32)  5.24 us
    dot_general x1, matrix products, local(): lax.dot_general(pair_cot, weight_fwd, (((1,), (1,)), ((), ())), preferred...  4.87 us
  transfers between devices with their start and end apart: 20, of which 12 were waited for; matrix products, arithmetic and copies ran while one was open for 21% of the time, Pallas kernels for 0%

profile of v1, /device:TPU:15, one launch (start us, length us, event | category | flops | bytes accessed | tf_op | source)
XLA Modules:
  0.0 207.4 jit_solution(13331869037245060146)
XLA Ops:
  7.2 0.7 all-gather.2.cloned.1.call-update
  8.2 0.1 eq.47
  8.4 0.1 eq.43
  8.6 0.1 mul.69
  8.8 0.9 reduce-window.6
  9.7 0.2 slice_reduce_fusion
  9.9 0.2 broadcast_in_dim.4
  10.1 0.3 reshape.177
  10.6 2.4 %scatter_custom_fusion = bf16[512,1024]{1,0:T(8,128)(2,1)S(1)} fusion(s32[384]{0:T(512)S(1)} %fusion.23, bf16[384,1024]{1,0:T(8,128)(2,1)S(1)} %reshape.177, bf16[]{:T(256)} %constant.106.clone.1), kind=kCustom, calls=%fused_computation.26 | custom fusion | bytes 1048578 | tf_op jit(solution)/shard_map/scatter | solution.py:61
  12.9 1.0 dynamic-slice_bitcast_fusion
  14.0 0.7 collective-permute-start.14
  14.6 0.3 collective-permute-start.13
  14.9 1.3 collective-permute-start.12
  16.2 3.3 %collective-permute-start.11 = (bf16[1,32,1024]{2,1,0:T(8,128)(2,1)}, bf16[1,32,1024]{2,1,0:T(8,128)(2,1)}, u32[]{:S(2)}, u32[]{:S(2)}) collective-permute-start(bf16[1,32,1024]{2,1,0:T(8,128)(2,1)} %get-tuple-element.9), channel_id=1, source_target_pairs={{0,12},{1,13},{2,14},{3,15},{4,0},{5,1},{6,2},{7,3},{8,4},{9,5},{1... | collective-permute-start | bytes 196616 | tf_op jit(solution)/shard_map/ppermute | solution.py:30
  19.5 1.5 collective-permute-start
  21.1 0.6 copy-done.2
  21.9 1.2 mul.76
  23.1 1.4 mul.77
  24.5 4.1 %scatter_custom_fusion.1 = bf16[512,1024]{1,0:T(8,128)(2,1)} fusion(s32[384]{0:T(512)S(1)} %fusion.23, f32[384,1024]{1,0:T(8,128)} %mul.77, f32[384]{0:T(512)S(1)} %mul.74, bf16[]{:T(256)} %constant.106.clone.1), kind=kCustom, calls=%fused_computation.23 | custom fusion | flops 786432 | bytes 2623490 | tf_op jit(solution)/shard_map/scatter | solution.py:64
  28.6 4.8 %all-to-all-start.1 = ((bf16[16,32,1024]{2,1,0:T(8,128)(2,1)}), bf16[16,32,1024]{2,1,0:T(8,128)(2,1)}, u32[]{:S(2)}, u32[]{:S(2)}) async-start(bf16[16,32,1024]{2,1,0:T(8,128)(2,1)} %bitcast.39), calls=%async_computation.1 | async-start | bytes 2097152 | tf_op jit(solution)/shard_map/all_to_all | solution.py:70
  33.5 1.2 collective-permute-start.1
  34.7 0.8 bitcast_dynamic-update-slice_fusion.14
  35.6 22.0 %collective-permute-done.1 = bf16[1,32,1024]{2,1,0:T(8,128)(2,1)S(1)} collective-permute-done((bf16[1,32,1024]{2,1,0:T(8,128)(2,1)S(1)}, bf16[1,32,1024]{2,1,0:T(8,128)(2,1)S(1)}, u32[]{:S(2)}, u32[]{:S(2)}) %collective-permute-start.1) | collective-permute-done | bytes 65568 | tf_op jit(solution)/shard_map/ppermute | solution.py:30
  57.6 4.0 %collective-permute-done.2 = bf16[1,32,1024]{2,1,0:T(8,128)(2,1)S(1)} collective-permute-done((bf16[1,32,1024]{2,1,0:T(8,128)(2,1)S(1)}, bf16[1,32,1024]{2,1,0:T(8,128)(2,1)S(1)}, u32[]{:S(2)}, u32[]{:S(2)}) %collective-permute-start.2) | collective-permute-done | bytes 65568 | tf_op jit(solution)/shard_map/ppermute | solution.py:30
  61.5 2.1 %collective-permute-start.3 = (bf16[1,32,1024]{2,1,0:T(8,128)(2,1)S(1)}, bf16[1,32,1024]{2,1,0:T(8,128)(2,1)S(1)}, u32[]{:S(2)}, u32[]{:S(2)}) collective-permute-start(bf16[1,32,1024]{2,1,0:T(8,128)(2,1)S(1)} %copy-done.12), channel_id=1, source_target_pairs={{0,4},{1,5},{2,6},{3,7},{4,8},{5,9},{6,10},{7,11},{8,12},{9,13},{1... | collective-permute-start | bytes 196616 | tf_op jit(solution)/shard_map/ppermute | solution.py:30
  63.6 1.4 collective-permute-done.3
  65.1 4.3 %collective-permute-start.4 = (bf16[1,32,1024]{2,1,0:T(8,128)(2,1)S(1)}, bf16[1,32,1024]{2,1,0:T(8,128)(2,1)S(1)}, u32[]{:S(2)}, u32[]{:S(2)}) collective-permute-start(bf16[1,32,1024]{2,1,0:T(8,128)(2,1)S(1)} %copy-done.11), channel_id=1, source_target_pairs={{0,5},{1,6},{2,7},{3,8},{4,9},{5,10},{6,11},{7,12},{8,13},{9,14},{... | collective-permute-start | bytes 196616 | tf_op jit(solution)/shard_map/ppermute | solution.py:30
  69.4 1.3 collective-permute-done.4
  70.7 2.1 %collective-permute-start.5 = (bf16[1,32,1024]{2,1,0:T(8,128)(2,1)S(1)}, bf16[1,32,1024]{2,1,0:T(8,128)(2,1)S(1)}, u32[]{:S(2)}, u32[]{:S(2)}) collective-permute-start(bf16[1,32,1024]{2,1,0:T(8,128)(2,1)S(1)} %copy-done.10), channel_id=1, source_target_pairs={{0,6},{1,7},{2,8},{3,9},{4,10},{5,11},{6,12},{7,13},{8,14},{9,15},... | collective-permute-start | bytes 196616 | tf_op jit(solution)/shard_map/ppermute | solution.py:30
  72.8 3.5 %collective-permute-done.5 = bf16[1,32,1024]{2,1,0:T(8,128)(2,1)S(1)} collective-permute-done((bf16[1,32,1024]{2,1,0:T(8,128)(2,1)S(1)}, bf16[1,32,1024]{2,1,0:T(8,128)(2,1)S(1)}, u32[]{:S(2)}, u32[]{:S(2)}) %collective-permute-start.5) | collective-permute-done | bytes 65568 | tf_op jit(solution)/shard_map/ppermute | solution.py:30
  76.3 2.5 %collective-permute-start.6 = (bf16[1,32,1024]{2,1,0:T(8,128)(2,1)S(1)}, bf16[1,32,1024]{2,1,0:T(8,128)(2,1)S(1)}, u32[]{:S(2)}, u32[]{:S(2)}) collective-permute-start(bf16[1,32,1024]{2,1,0:T(8,128)(2,1)S(1)} %copy-done.9), channel_id=1, source_target_pairs={{0,7},{1,8},{2,9},{3,10},{4,11},{5,12},{6,13},{7,14},{8,15},{9,0},... | collective-permute-start | bytes 196616 | tf_op jit(solution)/shard_map/ppermute | solution.py:30
  78.8 4.9 %collective-permute-done.6 = bf16[1,32,1024]{2,1,0:T(8,128)(2,1)S(1)} collective-permute-done((bf16[1,32,1024]{2,1,0:T(8,128)(2,1)S(1)}, bf16[1,32,1024]{2,1,0:T(8,128)(2,1)S(1)}, u32[]{:S(2)}, u32[]{:S(2)}) %collective-permute-start.6) | collective-permute-done | bytes 65568 | tf_op jit(solution)/shard_map/ppermute | solution.py:30
  83.8 0.6 collective-permute-start.7
  84.4 3.9 %collective-permute-done.7 = bf16[1,32,1024]{2,1,0:T(8,128)(2,1)S(1)} collective-permute-done((bf16[1,32,1024]{2,1,0:T(8,128)(2,1)S(1)}, bf16[1,32,1024]{2,1,0:T(8,128)(2,1)S(1)}, u32[]{:S(2)}, u32[]{:S(2)}) %collective-permute-start.7) | collective-permute-done | bytes 65568 | tf_op jit(solution)/shard_map/ppermute | solution.py:30
  88.3 3.8 %collective-permute-start.8 = (bf16[1,32,1024]{2,1,0:T(8,128)(2,1)S(1)}, bf16[1,32,1024]{2,1,0:T(8,128)(2,1)S(1)}, u32[]{:S(2)}, u32[]{:S(2)}) collective-permute-start(bf16[1,32,1024]{2,1,0:T(8,128)(2,1)S(1)} %copy-done.7), channel_id=1, source_target_pairs={{0,9},{1,10},{2,11},{3,12},{4,13},{5,14},{6,15},{7,0},{8,1},{9,2},... | collective-permute-start | bytes 196616 | tf_op jit(solution)/shard_map/ppermute | solution.py:30
  92.1 1.3 collective-permute-done.8
  93.4 3.7 %collective-permute-start.9 = (bf16[1,32,1024]{2,1,0:T(8,128)(2,1)S(1)}, bf16[1,32,1024]{2,1,0:T(8,128)(2,1)S(1)}, u32[]{:S(2)}, u32[]{:S(2)}) collective-permute-start(bf16[1,32,1024]{2,1,0:T(8,128)(2,1)S(1)} %copy-done.6), channel_id=1, source_target_pairs={{0,10},{1,11},{2,12},{3,13},{4,14},{5,15},{6,0},{7,1},{8,2},{9,3},... | collective-permute-start | bytes 196616 | tf_op jit(solution)/shard_map/ppermute | solution.py:30
  97.1 1.3 collective-permute-done.9
  98.4 5.1 %collective-permute-start.10 = (bf16[1,32,1024]{2,1,0:T(8,128)(2,1)S(1)}, bf16[1,32,1024]{2,1,0:T(8,128)(2,1)S(1)}, u32[]{:S(2)}, u32[]{:S(2)}) collective-permute-start(bf16[1,32,1024]{2,1,0:T(8,128)(2,1)S(1)} %copy-done.5), channel_id=1, source_target_pairs={{0,11},{1,12},{2,13},{3,14},{4,15},{5,0},{6,1},{7,2},{8,3},{9,4},{... | collective-permute-start | bytes 196616 | tf_op jit(solution)/shard_map/ppermute | solution.py:30
  103.6 3.9 %collective-permute-done.10 = bf16[1,32,1024]{2,1,0:T(8,128)(2,1)S(1)} collective-permute-done((bf16[1,32,1024]{2,1,0:T(8,128)(2,1)S(1)}, bf16[1,32,1024]{2,1,0:T(8,128)(2,1)S(1)}, u32[]{:S(2)}, u32[]{:S(2)}) %collective-permute-start.10) | collective-permute-done | bytes 65568 | tf_op jit(solution)/shard_map/ppermute | solution.py:30
  107.5 0.8 bitcast_dynamic-update-slice_fusion.3
  108.4 0.8 bitcast_dynamic-update-slice_fusion.2
  109.2 0.8 bitcast_dynamic-update-slice_fusion.1
  110.0 0.8 bitcast_dynamic-update-slice_fusion
  110.9 0.6 gather_fusion
  111.5 5.2 %fusion.2 = f32[512,1408]{1,0:T(8,128)} fusion(bf16[512,1024]{1,0:T(8,128)(2,1)S(1)} %bitcast.118, bf16[1,1024,1408]{2,1,0:T(8,128)(2,1)} %all-gather.2.cloned.1.call-done), kind=kOutput, calls=%fused_computation.8 | convolution fusion | flops 1476395008 | bytes 6815744 | tf_op jit(solution)/shard_map/dot_general | solution.py:75
  116.8 3.6 %multiply_convert_fusion.1 = (bf16[512,704]{1,0:T(8,128)(2,1)S(1)}, bf16[512,704]{1,0:T(8,128)(2,1)S(1)}) fusion(f32[512,1408]{1,0:T(8,128)} %fusion.2, bf16[512,1024]{1,0:T(8,128)(2,1)} %bitcast.40, bf16[1,704,1024]{2,1,0:T(8,128)(2,1)S(1)} %copy-done), kind=kOutput, calls=%fused_computation.12 | convolution fusion | flops 742883328 | bytes 6815744 | tf_op jit(solution)/shard_map/dot_general | solution.py:85
  120.4 0.9 copy-done.17
  121.3 0.3 copy-done.19
  121.6 3.5 %convolution_convert_fusion = bf16[1024,1408]{1,0:T(8,128)(2,1)} fusion(bf16[512,1024]{1,0:T(8,128)(2,1)S(1)} %bitcast.119, bf16[512,704]{1,0:T(8,128)(2,1)S(1)} %get-tuple-element.5, bf16[512,704]{1,0:T(8,128)(2,1)S(1)} %get-tuple-element.4), kind=kOutput, calls=%fused_computation.5 | convolution fusion | flops 1480720384 | bytes 5373952 | tf_op jit(solution)/shard_map/dot_general | solution.py:94
  125.1 3.9 %convolution_convert_fusion.1 = bf16[512,1024]{1,0:T(8,128)(2,1)} fusion(bf16[1,704,1024]{2,1,0:T(8,128)(2,1)S(1)} %copy-done, f32[512,1408]{1,0:T(8,128)} %fusion.2), kind=kOutput, calls=%fused_computation.18 | convolution fusion | flops 740884480 | bytes 5636096 | tf_op jit(solution)/shard_map/dot_general | solution.py:81
  129.0 6.5 %all-to-all-start = ((bf16[16,32,1024]{2,1,0:T(8,128)(2,1)}), bf16[16,32,1024]{2,1,0:T(8,128)(2,1)S(1)}, u32[]{:S(2)}, u32[]{:S(2)}) async-start(bf16[16,32,1024]{2,1,0:T(8,128)(2,1)} %bitcast.37), calls=%async_computation | async-start | bytes 2097152 | tf_op jit(solution)/shard_map/all_to_all | solution.py:98
  135.5 4.9 %fusion.5 = bf16[512,1024]{1,0:T(8,128)(2,1)} fusion(bf16[1,1024,1408]{2,1,0:T(8,128)(2,1)} %all-gather.2.cloned.1.call-done, bf16[512,704]{1,0:T(8,128)(2,1)} %copy-done.19, bf16[512,704]{1,0:T(8,128)(2,1)S(1)} %copy-done.18), kind=kOutput, calls=%fused_computation.17 | convolution fusion | flops 1479802880 | bytes 5373952 | tf_op jit(solution)/shard_map/dot_general | solution.py:91
  140.3 20.4 %all-to-all-done = bf16[16,32,1024]{2,1,0:T(8,128)(2,1)S(1)} async-done(((bf16[16,32,1024]{2,1,0:T(8,128)(2,1)}), bf16[16,32,1024]{2,1,0:T(8,128)(2,1)S(1)}, u32[]{:S(2)}, u32[]{:S(2)}) %all-to-all-start) | async-done | bytes 1048608 | tf_op jit(solution)/shard_map/all_to_all | solution.py:98
  160.7 4.5 %all-to-all-start.2 = ((bf16[16,32,1024]{2,1,0:T(8,128)(2,1)}), bf16[16,32,1024]{2,1,0:T(8,128)(2,1)S(1)}, u32[]{:S(2)}, u32[]{:S(2)}) async-start(bf16[16,32,1024]{2,1,0:T(8,128)(2,1)} %bitcast.120), calls=%async_computation.2 | async-start | bytes 2097152 | tf_op jit(solution)/shard_map/all_to_all | solution.py:105
  165.3 2.7 %gather_fusion.1 = bf16[384,1024]{1,0:T(8,128)(2,1)} fusion(bf16[512,1024]{1,0:T(8,128)(2,1)S(1)} %bitcast.114, s32[1024]{0:T(1024)S(1)} %pad_clamp_fusion), kind=kCustom, calls=%fused_computation.1 | custom fusion | bytes 1574400 | tf_op jit(solution)/shard_map/gather | solution.py:113
  168.0 22.2 %all-to-all-done.2 = bf16[16,32,1024]{2,1,0:T(8,128)(2,1)S(1)} async-done(((bf16[16,32,1024]{2,1,0:T(8,128)(2,1)}), bf16[16,32,1024]{2,1,0:T(8,128)(2,1)S(1)}, u32[]{:S(2)}, u32[]{:S(2)}) %all-to-all-start.2) | async-done | bytes 1048608 | tf_op jit(solution)/shard_map/all_to_all | solution.py:105
  190.2 2.7 %gather_fusion.2 = bf16[384,1024]{1,0:T(8,128)(2,1)} fusion(bf16[512,1024]{1,0:T(8,128)(2,1)S(1)} %bitcast.115, s32[1024]{0:T(1024)S(1)} %pad_clamp_fusion), kind=kCustom, calls=%fused_computation.2 | custom fusion | bytes 1574400 | tf_op jit(solution)/shard_map/gather | solution.py:116
  192.8 1.4 reshape.141
  194.2 0.7 fusion.16
  194.9 0.7 copy.23
  195.6 1.3 reshape.146
  197.0 1.4 reduce_sum.35
  198.3 2.2 %multiply_reduce_fusion = bf16[64,1024]{1,0:T(8,128)(2,1)} fusion(bf16[64,6,1024]{2,1,0:T(8,128)(2,1)S(1)} %reshape.141, f32[64,6]{1,0:T(8,128)} %copy-done.2), kind=kLoop, calls=%fused_computation.10 | loop fusion | flops 1114112 | bytes 919040 | tf_op jit(solution)/shard_map/reduce_sum | solution.py:119
  (71 shorter events, 0.9 us)
Async XLA Ops:
  7.2 109.6 %copy-start = (bf16[1,704,1024]{2,1,0:T(8,128)(2,1)S(1)}, bf16[1,704,1024]{2,1,0:T(8,128)(2,1)}, u32[]{:S(2)}) copy-start(bf16[1,704,1024]{2,1,0:T(8,128)(2,1)} %param.11) | copy-start | bytes 4325380
  7.2 1.0 copy-start.15
  7.2 2.7 %copy-start.3 = (bf16[64,1024]{1,0:T(8,128)(2,1)S(1)}, bf16[64,1024]{1,0:T(8,128)(2,1)}, u32[]{:S(2)}) copy-start(bf16[64,1024]{1,0:T(8,128)(2,1)} %param.6) | copy-start | bytes 393220
  7.2 104.3 %all-gather.2.cloned.1.call-start = ((), (), s32[]{:S(2)}) async-start(), calls=%async_computation.4 | async-start | bytes 4325376 | tf_op jit(solution)/shard_map/all_gather | solution.py:74
  10.6 10.5 %copy-start.16 = (f32[64,6]{0,1:T(8,128)S(1)}, f32[64,6]{0,1:T(8,128)}, u32[]{:S(2)}) copy-start(f32[64,6]{0,1:T(8,128)} %param.9) | copy-start | bytes 4612
  14.0 96.1 %collective-permute-start.14 = (bf16[1,32,1024]{2,1,0:T(8,128)(2,1)}, bf16[1,32,1024]{2,1,0:T(8,128)(2,1)}, u32[]{:S(2)}, u32[]{:S(2)}) collective-permute-start(bf16[1,32,1024]{2,1,0:T(8,128)(2,1)} %get-tuple-element.6), channel_id=1, source_target_pairs={{0,15},{1,0},{2,1},{3,2},{4,3},{5,4},{6,5},{7,6},{8,7},{9,8},{10,9... | collective-permute-start | bytes 196616 | tf_op jit(solution)/shard_map/ppermute | solution.py:30
  14.6 94.6 %collective-permute-start.13 = (bf16[1,32,1024]{2,1,0:T(8,128)(2,1)}, bf16[1,32,1024]{2,1,0:T(8,128)(2,1)}, u32[]{:S(2)}, u32[]{:S(2)}) collective-permute-start(bf16[1,32,1024]{2,1,0:T(8,128)(2,1)} %get-tuple-element.7), channel_id=1, source_target_pairs={{0,14},{1,15},{2,0},{3,1},{4,2},{5,3},{6,4},{7,5},{8,6},{9,7},{10,... | collective-permute-start | bytes 196616 | tf_op jit(solution)/shard_map/ppermute | solution.py:30
  14.9 93.5 %collective-permute-start.12 = (bf16[1,32,1024]{2,1,0:T(8,128)(2,1)}, bf16[1,32,1024]{2,1,0:T(8,128)(2,1)}, u32[]{:S(2)}, u32[]{:S(2)}) collective-permute-start(bf16[1,32,1024]{2,1,0:T(8,128)(2,1)} %get-tuple-element.8), channel_id=1, source_target_pairs={{0,13},{1,14},{2,15},{3,0},{4,1},{5,2},{6,3},{7,4},{8,5},{9,6},{10... | collective-permute-start | bytes 196616 | tf_op jit(solution)/shard_map/ppermute | solution.py:30
  16.2 91.3 %collective-permute-start.11 = (bf16[1,32,1024]{2,1,0:T(8,128)(2,1)}, bf16[1,32,1024]{2,1,0:T(8,128)(2,1)}, u32[]{:S(2)}, u32[]{:S(2)}) collective-permute-start(bf16[1,32,1024]{2,1,0:T(8,128)(2,1)} %get-tuple-element.9), channel_id=1, source_target_pairs={{0,12},{1,13},{2,14},{3,15},{4,0},{5,1},{6,2},{7,3},{8,4},{9,5},{1... | collective-permute-start | bytes 196616 | tf_op jit(solution)/shard_map/ppermute | solution.py:30
  19.5 14.0 %collective-permute-start = (bf16[1,32,1024]{2,1,0:T(8,128)(2,1)}, bf16[1,32,1024]{2,1,0:T(8,128)(2,1)}, u32[]{:S(2)}, u32[]{:S(2)}) collective-permute-start(bf16[1,32,1024]{2,1,0:T(8,128)(2,1)} %get-tuple-element.20), channel_id=1, source_target_pairs={{0,1},{1,2},{2,3},{3,4},{4,5},{5,6},{6,7},{7,8},{8,9},{9,10},{10,1... | collective-permute-start | bytes 196616 | tf_op jit(solution)/shard_map/ppermute | solution.py:30
  21.1 0.6 copy-start.2
  28.5 5.0 %copy-start.14 = (bf16[1,32,1024]{2,1,0:T(8,128)(2,1)S(1)}, bf16[1,32,1024]{2,1,0:T(8,128)(2,1)}, u32[]{:S(2)}) copy-start(bf16[1,32,1024]{2,1,0:T(8,128)(2,1)} %get-tuple-element.19) | copy-start | bytes 196612
  28.5 6.2 %copy-start.1 = (bf16[16,1,32,1024]{3,2,0,1:T(8,128)(2,1)S(1)}, bf16[16,1,32,1024]{3,2,0,1:T(8,128)(2,1)}, u32[]{:S(2)}) copy-start(bf16[16,1,32,1024]{3,2,0,1:T(8,128)(2,1)} %get-tuple-element.21) | copy-start | bytes 3145732
  28.5 29.0 %copy-start.13 = (bf16[1,32,1024]{2,1,0:T(8,128)(2,1)S(1)}, bf16[1,32,1024]{2,1,0:T(8,128)(2,1)}, u32[]{:S(2)}) copy-start(bf16[1,32,1024]{2,1,0:T(8,128)(2,1)} %get-tuple-element.18) | copy-start | bytes 196612
  28.5 33.0 %copy-start.12 = (bf16[1,32,1024]{2,1,0:T(8,128)(2,1)S(1)}, bf16[1,32,1024]{2,1,0:T(8,128)(2,1)}, u32[]{:S(2)}) copy-start(bf16[1,32,1024]{2,1,0:T(8,128)(2,1)} %get-tuple-element.17) | copy-start | bytes 196612
  28.5 36.5 %copy-start.11 = (bf16[1,32,1024]{2,1,0:T(8,128)(2,1)S(1)}, bf16[1,32,1024]{2,1,0:T(8,128)(2,1)}, u32[]{:S(2)}) copy-start(bf16[1,32,1024]{2,1,0:T(8,128)(2,1)} %get-tuple-element.16) | copy-start | bytes 196612
  28.5 42.2 %copy-start.10 = (bf16[1,32,1024]{2,1,0:T(8,128)(2,1)S(1)}, bf16[1,32,1024]{2,1,0:T(8,128)(2,1)}, u32[]{:S(2)}) copy-start(bf16[1,32,1024]{2,1,0:T(8,128)(2,1)} %get-tuple-element.15) | copy-start | bytes 196612
  28.6 47.8 %copy-start.9 = (bf16[1,32,1024]{2,1,0:T(8,128)(2,1)S(1)}, bf16[1,32,1024]{2,1,0:T(8,128)(2,1)}, u32[]{:S(2)}) copy-start(bf16[1,32,1024]{2,1,0:T(8,128)(2,1)} %get-tuple-element.14) | copy-start | bytes 196612
  28.6 55.2 %copy-start.8 = (bf16[1,32,1024]{2,1,0:T(8,128)(2,1)S(1)}, bf16[1,32,1024]{2,1,0:T(8,128)(2,1)}, u32[]{:S(2)}) copy-start(bf16[1,32,1024]{2,1,0:T(8,128)(2,1)} %get-tuple-element.13) | copy-start | bytes 196612
  28.6 59.7 %copy-start.7 = (bf16[1,32,1024]{2,1,0:T(8,128)(2,1)S(1)}, bf16[1,32,1024]{2,1,0:T(8,128)(2,1)}, u32[]{:S(2)}) copy-start(bf16[1,32,1024]{2,1,0:T(8,128)(2,1)} %get-tuple-element.12) | copy-start | bytes 196612
  28.6 64.8 %copy-start.6 = (bf16[1,32,1024]{2,1,0:T(8,128)(2,1)S(1)}, bf16[1,32,1024]{2,1,0:T(8,128)(2,1)}, u32[]{:S(2)}) copy-start(bf16[1,32,1024]{2,1,0:T(8,128)(2,1)} %get-tuple-element.11) | copy-start | bytes 196612
  28.6 69.8 %copy-start.5 = (bf16[1,32,1024]{2,1,0:T(8,128)(2,1)S(1)}, bf16[1,32,1024]{2,1,0:T(8,128)(2,1)}, u32[]{:S(2)}) copy-start(bf16[1,32,1024]{2,1,0:T(8,128)(2,1)} %get-tuple-element.10) | copy-start | bytes 196612
  28.6 88.2 %all-to-all-start.1 = ((bf16[16,32,1024]{2,1,0:T(8,128)(2,1)}), bf16[16,32,1024]{2,1,0:T(8,128)(2,1)}, u32[]{:S(2)}, u32[]{:S(2)}) async-start(bf16[16,32,1024]{2,1,0:T(8,128)(2,1)} %bitcast.39), calls=%async_computation.1 | async-start | bytes 2097152 | tf_op jit(solution)/shard_map/all_to_all | solution.py:70
  33.4 167.1 %reduce-scatter.2.cloned.1.call-start = ((), (), s32[]{:S(2)}) async-start(), calls=%async_computation.5 | async-start | bytes 4325376 | tf_op jit(solution)/shard_map/reduce_scatter | solution.py:124
  33.5 24.1 %collective-permute-start.1 = (bf16[1,32,1024]{2,1,0:T(8,128)(2,1)S(1)}, bf16[1,32,1024]{2,1,0:T(8,128)(2,1)S(1)}, u32[]{:S(2)}, u32[]{:S(2)}) collective-permute-start(bf16[1,32,1024]{2,1,0:T(8,128)(2,1)S(1)} %copy-done.14), channel_id=1, source_target_pairs={{0,2},{1,3},{2,4},{3,5},{4,6},{5,7},{6,8},{7,9},{8,10},{9,11},{10,... | collective-permute-start | bytes 196616 | tf_op jit(solution)/shard_map/ppermute | solution.py:30
  57.5 4.0 %collective-permute-start.2 = (bf16[1,32,1024]{2,1,0:T(8,128)(2,1)S(1)}, bf16[1,32,1024]{2,1,0:T(8,128)(2,1)S(1)}, u32[]{:S(2)}, u32[]{:S(2)}) collective-permute-start(bf16[1,32,1024]{2,1,0:T(8,128)(2,1)S(1)} %copy-done.13), channel_id=1, source_target_pairs={{0,3},{1,4},{2,5},{3,6},{4,7},{5,8},{6,9},{7,10},{8,11},{9,12},{10... | collective-permute-start | bytes 196616 | tf_op jit(solution)/shard_map/ppermute | solution.py:30
  61.5 3.5 %collective-permute-start.3 = (bf16[1,32,1024]{2,1,0:T(8,128)(2,1)S(1)}, bf16[1,32,1024]{2,1,0:T(8,128)(2,1)S(1)}, u32[]{:S(2)}, u32[]{:S(2)}) collective-permute-start(bf16[1,32,1024]{2,1,0:T(8,128)(2,1)S(1)} %copy-done.12), channel_id=1, source_target_pairs={{0,4},{1,5},{2,6},{3,7},{4,8},{5,9},{6,10},{7,11},{8,12},{9,13},{1... | collective-permute-start | bytes 196616 | tf_op jit(solution)/shard_map/ppermute | solution.py:30
  65.1 5.6 %collective-permute-start.4 = (bf16[1,32,1024]{2,1,0:T(8,128)(2,1)S(1)}, bf16[1,32,1024]{2,1,0:T(8,128)(2,1)S(1)}, u32[]{:S(2)}, u32[]{:S(2)}) collective-permute-start(bf16[1,32,1024]{2,1,0:T(8,128)(2,1)S(1)} %copy-done.11), channel_id=1, source_target_pairs={{0,5},{1,6},{2,7},{3,8},{4,9},{5,10},{6,11},{7,12},{8,13},{9,14},{... | collective-permute-start | bytes 196616 | tf_op jit(solution)/shard_map/ppermute | solution.py:30
  70.7 5.6 %collective-permute-start.5 = (bf16[1,32,1024]{2,1,0:T(8,128)(2,1)S(1)}, bf16[1,32,1024]{2,1,0:T(8,128)(2,1)S(1)}, u32[]{:S(2)}, u32[]{:S(2)}) collective-permute-start(bf16[1,32,1024]{2,1,0:T(8,128)(2,1)S(1)} %copy-done.10), channel_id=1, source_target_pairs={{0,6},{1,7},{2,8},{3,9},{4,10},{5,11},{6,12},{7,13},{8,14},{9,15},... | collective-permute-start | bytes 196616 | tf_op jit(solution)/shard_map/ppermute | solution.py:30
  76.3 7.4 %collective-permute-start.6 = (bf16[1,32,1024]{2,1,0:T(8,128)(2,1)S(1)}, bf16[1,32,1024]{2,1,0:T(8,128)(2,1)S(1)}, u32[]{:S(2)}, u32[]{:S(2)}) collective-permute-start(bf16[1,32,1024]{2,1,0:T(8,128)(2,1)S(1)} %copy-done.9), channel_id=1, source_target_pairs={{0,7},{1,8},{2,9},{3,10},{4,11},{5,12},{6,13},{7,14},{8,15},{9,0},... | collective-permute-start | bytes 196616 | tf_op jit(solution)/shard_map/ppermute | solution.py:30
  83.8 4.5 %collective-permute-start.7 = (bf16[1,32,1024]{2,1,0:T(8,128)(2,1)S(1)}, bf16[1,32,1024]{2,1,0:T(8,128)(2,1)S(1)}, u32[]{:S(2)}, u32[]{:S(2)}) collective-permute-start(bf16[1,32,1024]{2,1,0:T(8,128)(2,1)S(1)} %copy-done.8), channel_id=1, source_target_pairs={{0,8},{1,9},{2,10},{3,11},{4,12},{5,13},{6,14},{7,15},{8,0},{9,1},... | collective-permute-start | bytes 196616 | tf_op jit(solution)/shard_map/ppermute | solution.py:30
  88.3 5.1 %collective-permute-start.8 = (bf16[1,32,1024]{2,1,0:T(8,128)(2,1)S(1)}, bf16[1,32,1024]{2,1,0:T(8,128)(2,1)S(1)}, u32[]{:S(2)}, u32[]{:S(2)}) collective-permute-start(bf16[1,32,1024]{2,1,0:T(8,128)(2,1)S(1)} %copy-done.7), channel_id=1, source_target_pairs={{0,9},{1,10},{2,11},{3,12},{4,13},{5,14},{6,15},{7,0},{8,1},{9,2},... | collective-permute-start | bytes 196616 | tf_op jit(solution)/shard_map/ppermute | solution.py:30
  93.4 5.0 %collective-permute-start.9 = (bf16[1,32,1024]{2,1,0:T(8,128)(2,1)S(1)}, bf16[1,32,1024]{2,1,0:T(8,128)(2,1)S(1)}, u32[]{:S(2)}, u32[]{:S(2)}) collective-permute-start(bf16[1,32,1024]{2,1,0:T(8,128)(2,1)S(1)} %copy-done.6), channel_id=1, source_target_pairs={{0,10},{1,11},{2,12},{3,13},{4,14},{5,15},{6,0},{7,1},{8,2},{9,3},... | collective-permute-start | bytes 196616 | tf_op jit(solution)/shard_map/ppermute | solution.py:30
  98.4 9.1 %collective-permute-start.10 = (bf16[1,32,1024]{2,1,0:T(8,128)(2,1)S(1)}, bf16[1,32,1024]{2,1,0:T(8,128)(2,1)S(1)}, u32[]{:S(2)}, u32[]{:S(2)}) collective-permute-start(bf16[1,32,1024]{2,1,0:T(8,128)(2,1)S(1)} %copy-done.5), channel_id=1, source_target_pairs={{0,11},{1,12},{2,13},{3,14},{4,15},{5,0},{6,1},{7,2},{8,3},{9,4},{... | collective-permute-start | bytes 196616 | tf_op jit(solution)/shard_map/ppermute | solution.py:30
  120.4 0.9 copy-start.17
  120.4 1.1 copy-start.19
  129.0 6.5 %copy-start.18 = (bf16[512,704]{1,0:T(8,128)(2,1)S(1)}, bf16[512,704]{1,0:T(8,128)(2,1)}, u32[]{:S(2)}) copy-start(bf16[512,704]{1,0:T(8,128)(2,1)} %copy-done.17) | copy-start | bytes 2162692
  129.0 31.7 %all-to-all-start = ((bf16[16,32,1024]{2,1,0:T(8,128)(2,1)}), bf16[16,32,1024]{2,1,0:T(8,128)(2,1)S(1)}, u32[]{:S(2)}, u32[]{:S(2)}) async-start(bf16[16,32,1024]{2,1,0:T(8,128)(2,1)} %bitcast.37), calls=%async_computation | async-start | bytes 2097152 | tf_op jit(solution)/shard_map/all_to_all | solution.py:98
  160.7 29.4 %all-to-all-start.2 = ((bf16[16,32,1024]{2,1,0:T(8,128)(2,1)}), bf16[16,32,1024]{2,1,0:T(8,128)(2,1)S(1)}, u32[]{:S(2)}, u32[]{:S(2)}) async-start(bf16[16,32,1024]{2,1,0:T(8,128)(2,1)} %bitcast.120), calls=%async_computation.2 | async-start | bytes 2097152 | tf_op jit(solution)/shard_map/all_to_all | solution.py:105
  192.8 1.4 copy-start.4
Sparse Core Ops, SparseCore 0:
  9.6 42.1 all-gather.1
  125.2 40.4 reduce-scatter.1
